TPU v7x, 256 devices: a whole 4x4x8 slice. The times are simulated.
256 devices in a mesh: row: 16 (over z, core), col: 16 (over x, y).
Axes of the slice: x: 4, y: 4, z: 8, core: 2. Of those that a mesh axis runs over, the one named last changes fastest.
Arguments:
- site_tensor: bfloat16 [1024, 4, 1024], P('row', None, 'col'), may hold values from -180 to 180
- site_tangent: bfloat16 [1024, 4, 1024], P('row', None, 'col'), may hold values from -180 to 180
- left_env: bfloat16 [1024, 16384], P('row', 'col'), may hold values from -0.1875 to 0.375
- right_env: bfloat16 [1024, 16384], P('row', 'col'), may hold values from -0.046875 to 0.09375
- mpo: bfloat16 [16, 16, 4, 4], replicated, may hold values from -0.25 to 0.75
- dissipation: float32 [4], replicated, may hold values from 0.2 to 2
Outputs:
- evolved: float32 [1024, 4, 1024], P('row', None, 'col')
- evolved_tangent: float32 [1024, 4, 1024], P('row', None, 'col')
All inputs are finite; a program needn't handle non-finite values.
Results may differ from a plain program's by a relative error of at most 0.0055.
Values may be sent and summed in bfloat16 or wider, within the bound.
No kernel may reach another device: no remote copies, remote signals or barrier semaphores. Data moves between devices by JAX's collectives and lax.ppermute only.
A program may use at most 64 MiB of HBM per device.

v0:
```python
import jax
import jax.numpy as jnp
from jax import lax
from jax.sharding import PartitionSpec as P

KRYLOV = 3
taylor_order = 16


def inner(first, second):
    return jnp.sum(first * second)


def taylor(hess, dhess):
    size = hess.shape[0]
    term = jnp.zeros((size,), jnp.float32).at[0].set(1.0)
    dterm = jnp.zeros((size,), jnp.float32)
    total = term
    dtotal = dterm
    for order in range(1, taylor_order + 1):
        nterm = jnp.dot(hess, term, precision=lax.Precision.HIGHEST) / order
        dterm = (
            jnp.dot(dhess, term, precision=lax.Precision.HIGHEST)
            + jnp.dot(hess, dterm, precision=lax.Precision.HIGHEST)
        ) / order
        term = nterm
        total = total + term
        dtotal = dtotal + dterm
    return (total, dtotal)


def local(site_tensor, site_tangent, left_env, right_env, mpo, dissipation):
    rows_here, physical, cols_here = site_tensor.shape
    channels = mpo.shape[0]
    left_whole = lax.all_gather(left_env, "col", axis=1, tiled=True)
    right_whole = lax.all_gather(right_env, "row", axis=0, tiled=True)

    def apply(stacked):
        panels = stacked.shape[1]
        whole = lax.all_gather(stacked.astype(jnp.bfloat16), "row", axis=0, tiled=True)
        flat = whole.reshape(whole.shape[0], panels * physical * cols_here)
        left_three = left_whole.reshape(rows_here, flat.shape[0], channels)
        mixed = lax.dot_general(
            left_three, flat, (((1,), (0,)), ((), ())), preferred_element_type=jnp.float32
        )
        mixed = mixed.astype(jnp.bfloat16).reshape(rows_here, channels, panels, physical, cols_here)
        channel = jnp.einsum("awspr,wvpq->asqrv", mixed, mpo, preferred_element_type=jnp.float32)
        channel = channel.astype(jnp.bfloat16).reshape(
            rows_here * panels * physical, cols_here * channels
        )
        partial_rows = lax.dot_general(
            channel, right_whole, (((1,), (1,)), ((), ())), preferred_element_type=jnp.float32
        )
        partial_rows = partial_rows.reshape(rows_here, panels, physical, partial_rows.shape[1])
        summed = lax.psum_scatter(partial_rows, "col", scatter_dimension=3, tiled=True)
        return summed - dissipation[None, None, :, None] * stacked

    primal = site_tensor.astype(jnp.float32)
    tangent = site_tangent.astype(jnp.float32)
    starting = lax.psum(jnp.stack([inner(primal, primal), inner(primal, tangent)]), ("row", "col"))
    norm_site = jnp.sqrt(starting[0])
    norm_tangent = starting[1] / norm_site
    basis = [primal / norm_site]
    tangents = [(tangent - basis[0] * norm_tangent) / norm_site]
    hess = jnp.zeros((KRYLOV, KRYLOV), jnp.float32)
    dhess = jnp.zeros((KRYLOV, KRYLOV), jnp.float32)
    for level in range(KRYLOV):
        image = apply(basis[level][:, None])[:, 0]
        dimage = apply(tangents[level][:, None])[:, 0]
        counted = level + 1
        locals_list = [inner(vector, image) for vector in basis]
        locals_list = locals_list + [inner(vector, image) for vector in tangents]
        locals_list = locals_list + [inner(vector, dimage) for vector in basis]
        totals = lax.psum(jnp.stack(locals_list), ("row", "col"))
        coeffs = totals[:counted]
        across = totals[counted : 2 * counted]
        along = totals[2 * counted : 3 * counted]
        dcoeffs = across + along
        hess = hess.at[:counted, level].set(coeffs)
        dhess = dhess.at[:counted, level].set(dcoeffs)
        if level + 1 < KRYLOV:
            residual = image
            dresidual = dimage
            for index in range(counted):
                residual = residual - coeffs[index] * basis[index]
                dresidual = (
                    dresidual - dcoeffs[index] * basis[index] - coeffs[index] * tangents[index]
                )
            paired = lax.psum(
                jnp.stack([inner(residual, residual), inner(residual, dresidual)]), ("row", "col")
            )
            squared = paired[0]
            mixed_term = paired[1]
            height = jnp.sqrt(squared)
            dheight = mixed_term / height
            newvec = residual / height
            basis.append(newvec)
            tangents.append((dresidual - newvec * dheight) / height)
            hess = hess.at[level + 1, level].set(height)
            dhess = dhess.at[level + 1, level].set(dheight)
    coeff, dcoeff = taylor(hess, dhess)
    spread = jnp.zeros_like(primal)
    dspread = jnp.zeros_like(primal)
    for index in range(KRYLOV):
        spread = spread + coeff[index] * basis[index]
        dspread = dspread + coeff[index] * tangents[index] + dcoeff[index] * basis[index]
    evolved = norm_site * spread
    evolved_tangent = norm_tangent * spread + norm_site * dspread
    return (evolved, evolved_tangent)


def solution(mesh):
    in_specs = (
        P("row", None, "col"),
        P("row", None, "col"),
        P("row", "col"),
        P("row", "col"),
        P(),
        P(),
    )
    out_specs = (P("row", None, "col"), P("row", None, "col"))
    return jax.shard_map(local, mesh=mesh, in_specs=in_specs, out_specs=out_specs, check_vma=False)
```

profile of v0, /device:TPU:1, one launch (start us, length us, event | category | flops | bytes accessed | tf_op | source)
XLA Modules:
  0.0 1113.4 jit_solution(7619003044250572234)
XLA Ops:
  11.6 81.9 %psum.42 = f32[2]{0:T(128)S(1)} all-reduce(f32[2]{0:T(128)S(1)} %pad_maximum_fusion), channel_id=1, replica_groups=mesh['row'=16,'col'=16] {'row','col'}, use_global_device_ids=true, to_apply=%region_2.0 | all-reduce | flops 2 | bytes 16 | tf_op jit(solution)/shard_map/psum | solution.py:60
  96.4 18.8 %all-gather = bf16[1024,4,64]{2,1,0:T(4,128)(2,1)S(1)} all-gather(bf16[64,4,64]{2,1,0:T(4,128)(2,1)S(1)} %get-tuple-element.182), channel_id=2, replica_groups=mesh['row'=16,'col'=16] {'row'}, dimensions={0}, use_global_device_ids=true | all-gather | bytes 557056 | tf_op jit(solution)/shard_map/all_gather | solution.py:40
  116.0 4.8 copy.120
  120.8 4.5 copy.122
  137.6 18.6 %all-gather.1 = bf16[1024,4,64]{2,1,0:T(4,128)(2,1)S(1)} all-gather(bf16[64,4,64]{2,1,0:T(4,128)(2,1)S(1)} %get-tuple-element.181), channel_id=3, replica_groups=mesh['row'=16,'col'=16] {'row'}, dimensions={0}, use_global_device_ids=true | all-gather | bytes 557056 | tf_op jit(solution)/shard_map/all_gather | solution.py:40
  161.8 3.6 copy.133
  173.1 37.3 %reduce-scatter.19.cloned.1.call-done = f32[64,256]{1,0:T(8,128)} async-done(((f32[1024,256]{1,0:T(8,128)}), f32[64,256]{1,0:T(8,128)}) %reduce-scatter.19.cloned.1.call-update) | async-done | bytes 65552
  211.4 80.8 %reduce-scatter.21.cloned.1.call-done = f32[64,256]{1,0:T(8,128)} async-done(((f32[1024,256]{1,0:T(8,128)}), f32[64,256]{1,0:T(8,128)}) %reduce-scatter.21.cloned.1.call-update) | async-done | bytes 65552
  296.1 77.2 %psum.43 = f32[3]{0:T(128)S(1)} all-reduce(f32[3]{0:T(128)S(1)} %pad_maximum_fusion.1), channel_id=1, replica_groups=mesh['row'=16,'col'=16] {'row','col'}, use_global_device_ids=true, to_apply=%region_8.0 | all-reduce | flops 3 | bytes 24 | tf_op jit(solution)/shard_map/psum | solution.py:74
  378.1 73.2 %psum.44 = f32[2]{0:T(128)S(1)} all-reduce(f32[2]{0:T(128)S(1)} %pad_maximum_fusion.2), channel_id=1, replica_groups=mesh['row'=16,'col'=16] {'row','col'}, use_global_device_ids=true, to_apply=%region_11.0 | all-reduce | flops 2 | bytes 16 | tf_op jit(solution)/shard_map/psum | solution.py:89
  453.9 18.9 %all-gather.2 = bf16[1024,4,64]{2,1,0:T(4,128)(2,1)S(1)} all-gather(bf16[64,4,64]{2,1,0:T(4,128)(2,1)S(1)} %get-tuple-element.180), channel_id=4, replica_groups=mesh['row'=16,'col'=16] {'row'}, dimensions={0}, use_global_device_ids=true | all-gather | bytes 557056 | tf_op jit(solution)/shard_map/all_gather | solution.py:40
  474.1 3.3 fusion.38
  482.2 3.6 copy.141
  493.5 18.4 %all-gather.3 = bf16[1024,4,64]{2,1,0:T(4,128)(2,1)S(1)} all-gather(bf16[64,4,64]{2,1,0:T(4,128)(2,1)} %get-tuple-element.173), channel_id=5, replica_groups=mesh['row'=16,'col'=16] {'row'}, dimensions={0}, use_global_device_ids=true | all-gather | bytes 557056 | tf_op jit(solution)/shard_map/all_gather | solution.py:40
  513.3 3.3 fusion.39
  521.4 3.6 copy.149
  532.6 33.9 %reduce-scatter.23.cloned.1.call-done = f32[64,256]{1,0:T(8,128)} async-done(((f32[1024,256]{1,0:T(8,128)}), f32[64,256]{1,0:T(8,128)}) %reduce-scatter.23.cloned.1.call-update) | async-done | bytes 65552
  567.6 80.8 %reduce-scatter.25.cloned.1.call-done = f32[64,256]{1,0:T(8,128)} async-done(((f32[1024,256]{1,0:T(8,128)}), f32[64,256]{1,0:T(8,128)}) %reduce-scatter.25.cloned.1.call-update) | async-done | bytes 65552
  650.4 3.9 stack.106
  654.3 77.2 %psum.45 = f32[6]{0:T(128)S(1)} all-reduce(f32[6]{0:T(128)S(1)} %stack.106), channel_id=1, replica_groups=mesh['row'=16,'col'=16] {'row','col'}, use_global_device_ids=true, to_apply=%region_20.0 | all-reduce | flops 6 | bytes 48 | tf_op jit(solution)/shard_map/psum | solution.py:74
  732.8 3.4 multiply_reduce_fusion.1
  737.5 73.3 %psum.46 = f32[2]{0:T(128)S(1)} all-reduce(f32[2]{0:T(128)S(1)} %pad_maximum_fusion.3), channel_id=1, replica_groups=mesh['row'=16,'col'=16] {'row','col'}, use_global_device_ids=true, to_apply=%region_23.0 | all-reduce | flops 2 | bytes 16 | tf_op jit(solution)/shard_map/psum | solution.py:89
  813.4 18.9 %all-gather.5 = bf16[1024,4,64]{2,1,0:T(4,128)(2,1)S(1)} all-gather(bf16[64,4,64]{2,1,0:T(4,128)(2,1)S(1)} %get-tuple-element.168), channel_id=7, replica_groups=mesh['row'=16,'col'=16] {'row'}, dimensions={0}, use_global_device_ids=true | all-gather | bytes 557056 | tf_op jit(solution)/shard_map/all_gather | solution.py:40
  841.8 3.6 copy.165
  853.1 18.5 %all-gather.4 = bf16[1024,4,64]{2,1,0:T(4,128)(2,1)S(1)} all-gather(bf16[64,4,64]{2,1,0:T(4,128)(2,1)} %get-tuple-element.179), channel_id=6, replica_groups=mesh['row'=16,'col'=16] {'row'}, dimensions={0}, use_global_device_ids=true | all-gather | bytes 557056 | tf_op jit(solution)/shard_map/all_gather | solution.py:40
  872.9 3.3 fusion.40
  881.1 3.6 copy.157
  894.8 31.1 %reduce-scatter.29.cloned.1.call-done = f32[64,256]{1,0:T(8,128)} async-done(((f32[1024,256]{1,0:T(8,128)}), f32[64,256]{1,0:T(8,128)}) %reduce-scatter.29.cloned.1.call-update) | async-done | bytes 65552
  927.0 80.9 %reduce-scatter.27.cloned.1.call-done = f32[64,256]{1,0:T(8,128)} async-done(((f32[1024,256]{1,0:T(8,128)}), f32[64,256]{1,0:T(8,128)}) %reduce-scatter.27.cloned.1.call-update) | async-done | bytes 65552
  1010.3 5.8 stack.119
  1016.2 77.2 %psum.47 = f32[9]{0:T(128)S(1)} all-reduce(f32[9]{0:T(128)S(1)} %stack.119), channel_id=1, replica_groups=mesh['row'=16,'col'=16] {'row','col'}, use_global_device_ids=true, to_apply=%region_35.0 | all-reduce | flops 9 | bytes 72 | tf_op jit(solution)/shard_map/psum | solution.py:74
  1101.5 4.5 multiply_add_fusion
  (179 shorter events, 121.0 us)
Async XLA Ops:
  7.2 108.7 %copy-start.8 = (bf16[16,16,4,4]{1,3,2,0:T(4,128)(2,1)S(1)}, bf16[16,16,4,4]{1,3,2,0:T(4,128)(2,1)}, u32[]{:S(2)}) copy-start(bf16[16,16,4,4]{1,3,2,0:T(4,128)(2,1)} %param.32) | copy-start | bytes 24580
  7.2 108.9 %all-gather.9.cloned.1.call-start = ((), (), s32[]{:S(2)}) async-start(), calls=%async_computation.6 | async-start | bytes 2228224 | tf_op jit(solution)/shard_map/all_gather | solution.py:35
  7.9 123.7 %all-gather.11.cloned.1.call-start = ((), (), s32[]{:S(2)}) async-start(), calls=%async_computation.7 | async-start | bytes 2228224 | tf_op jit(solution)/shard_map/all_gather | solution.py:36
  8.7 201.7 %reduce-scatter.19.cloned.1.call-start = ((), (), s32[]{:S(2)}) async-start(), calls=%async_computation.8 | async-start | bytes 1114112
  116.0 43.8 %copy-start.9 = (bf16[16,16,4,4]{0,1,2,3:T(8,128)(2,1)}, bf16[16,16,4,4]{0,1,2,3:T(8,128)(2,1)S(1)}, u32[]{:S(2)}) copy-start(bf16[16,16,4,4]{0,1,2,3:T(8,128)(2,1)S(1)} %copy.124) | copy-start | bytes 24580
  125.3 3.6 copy-start.5
  137.6 20.1 %copy-start.6 = (bf16[64,1024,16]{1,0,2:T(8,128)(2,1)S(1)}, bf16[64,1024,16]{1,0,2:T(8,128)(2,1)}, u32[]{:S(2)}) copy-start(bf16[64,1024,16]{1,0,2:T(8,128)(2,1)} %copy-done.5) | copy-start | bytes 6291460
  137.6 154.6 %reduce-scatter.21.cloned.1.call-start = ((), (), s32[]{:S(2)}) async-start(), calls=%async_computation.9 | async-start | bytes 1114112
  159.9 5.6 copy-start
  169.7 123.6 %copy-start.1 = (bf16[64,4,64]{2,1,0:T(4,128)(2,1)S(1)}, bf16[64,4,64]{2,1,0:T(4,128)(2,1)}, u32[]{:S(2)}) copy-start(bf16[64,4,64]{2,1,0:T(4,128)(2,1)} %param.28) | copy-start | bytes 98308
  169.7 123.6 %copy-start.2 = (bf16[64,4,64]{2,1,0:T(4,128)(2,1)S(1)}, bf16[64,4,64]{2,1,0:T(4,128)(2,1)}, u32[]{:S(2)}) copy-start(bf16[64,4,64]{2,1,0:T(4,128)(2,1)} %param.29) | copy-start | bytes 98308
  169.7 123.6 %copy-start.10 = (f32[4]{0:T(128)S(1)}, f32[4]{0:T(128)}, u32[]{:S(2)}) copy-start(f32[4]{0:T(128)} %param.33) | copy-start | bytes 52
  173.0 393.5 %reduce-scatter.23.cloned.1.call-start = ((), (), s32[]{:S(2)}) async-start(), calls=%async_computation.10 | async-start | bytes 1114112
  493.4 154.9 %reduce-scatter.25.cloned.1.call-start = ((), (), s32[]{:S(2)}) async-start(), calls=%async_computation.11 | async-start | bytes 1114112
  532.6 393.4 %reduce-scatter.29.cloned.1.call-start = ((), (), s32[]{:S(2)}) async-start(), calls=%async_computation.13 | async-start | bytes 1114112
  736.2 77.2 %copy-start.3 = (f32[64,4,64]{2,1,0:T(4,128)}, f32[64,4,64]{2,1,0:T(4,128)S(1)}, u32[]{:S(2)}) copy-start(f32[64,4,64]{2,1,0:T(4,128)S(1)} %get-tuple-element.171) | copy-start | bytes 196612
  853.0 155.0 %reduce-scatter.27.cloned.1.call-start = ((), (), s32[]{:S(2)}) async-start(), calls=%async_computation.12 | async-start | bytes 1114112
  888.2 120.9 %copy-start.4 = (f32[64,4,64]{2,1,0:T(4,128)S(1)}, f32[64,4,64]{2,1,0:T(4,128)}, u32[]{:S(2)}) copy-start(f32[64,4,64]{2,1,0:T(4,128)} %copy-done.3) | copy-start | bytes 196612
  888.2 120.9 %copy-start.7 = (f32[64,4,64]{2,1,0:T(4,128)S(1)}, f32[64,4,64]{2,1,0:T(4,128)}, u32[]{:S(2)}) copy-start(f32[64,4,64]{2,1,0:T(4,128)} %get-tuple-element.169) | copy-start | bytes 196612
  890.3 203.3 %copy-start.11 = (f32[3,1]{0,1:T(1,128)S(1)}, f32[3,1]{0,1:T(1,128)}, u32[]{:S(2)}) copy-start(f32[3,1]{0,1:T(1,128)} %constant.327) | copy-start | bytes 40
Sparse Core Ops, SparseCore 0:
  10.5 52.1 all-gather.8
  64.5 40.9 all-gather.10
  137.7 72.6 reduce-scatter.18
  213.7 78.4 reduce-scatter.20
  493.6 72.8 reduce-scatter.22
  569.8 78.4 reduce-scatter.24
  853.1 72.8 reduce-scatter.28
  929.5 78.4 reduce-scatter.26
where the time goes:
time: 1120 us; the launch traced here: 1110 us
  blocking collectives  572 us (51%)
  waiting for transfers between devices  346 us (31%)
  local copies, waits for them, and re-layouts  98.9 us (9%)
  matrix products  52.6 us (5%)
  other arithmetic  22.7 us (2%)
  between operations  20.4 us (2%)
    unnamed x14, waiting for transfers between devices  346 us
    psum x3, blocking collectives, local(): totals = lax.psum(jnp.stack(locals_list), ('row', 'col'))  232 us
    psum x2, blocking collectives, local(): lax.psum(jnp.stack([inner(residual, residual), inner(residual, dresidual)...  146 us
    all_gather x6, blocking collectives, apply(): lax.all_gather(stacked.astype(jnp.bfloat16), 'row', axis=0, tiled=True)  112 us
    psum x1, blocking collectives, local(): lax.psum(jnp.stack([inner(primal, primal), inner(primal, tangent)]), ('ro...  81.9 us
    unnamed x43, local copies, waits for them, and re-layouts  31.9 us
  transfers between devices with their start and end apart: 8, of which 6 were waited for; matrix products, arithmetic and copies ran while one was open for 8% of the time, Pallas kernels for 0%

commit v1 on v0

--- a/solution.py
+++ b/solution.py
@@ -37,7 +37,12 @@
 
     def apply(stacked):
         panels = stacked.shape[1]
-        whole = lax.all_gather(stacked.astype(jnp.bfloat16), "row", axis=0, tiled=True)
+        whole = jnp.concatenate(
+            lax.all_to_all(
+                jnp.stack([stacked.astype(jnp.bfloat16)] * lax.axis_size("row")), "row", 0, 0
+            ),
+            axis=0,
+        )
         flat = whole.reshape(whole.shape[0], panels * physical * cols_here)
         left_three = left_whole.reshape(rows_here, flat.shape[0], channels)
         mixed = lax.dot_general(

time: 1120 us -> 1140 us (1.018)
  local copies, waits for them, and re-layouts: 98.9 us -> 127 us
    all_gather x6 -> x0, blocking collectives: 112 us -> none  [apply(): lax.all_gather(stacked.astype(jnp.bfloat16), 'row', axis=0, tiled=True)]
    all_to_all x0 -> x5, blocking collectives: none -> 108 us  [apply(): lax.all_to_all(jnp.stack([stacked.astype(jnp.bfloat16)] * lax.axis_size('...]
    unnamed x43 -> x73, local copies, waits for them, and re-layouts: 31.9 us -> 59.9 us
    unnamed x14, waiting for transfers between devices: 346 us -> 319 us
    all_to_all x0 -> x1, waiting for transfers between devices: none -> 17 us  [apply(): lax.all_to_all(jnp.stack([stacked.astype(jnp.bfloat16)] * lax.axis_size('...]
  transfers between devices with their start and end apart: 8 -> 9, of which waited for: 6 -> 7; matrix products, arithmetic and copies ran while one was open for 8% -> 9% of each run, Pallas kernels for 0% -> 0%
where the time goes in v1:
time: 1140 us; the launch traced here: 1130 us
  blocking collectives  568 us (50%)
  waiting for transfers between devices  336 us (29%)
  local copies, waits for them, and re-layouts  127 us (11%)
  matrix products  52.4 us (5%)
  other arithmetic  21.1 us (2%)
  between operations  20.5 us (2%)
    unnamed x14, waiting for transfers between devices  319 us
    psum x3, blocking collectives, local(): totals = lax.psum(jnp.stack(locals_list), ('row', 'col'))  232 us
    psum x2, blocking collectives, local(): lax.psum(jnp.stack([inner(residual, residual), inner(residual, dresidual)...  147 us
    all_to_all x5, blocking collectives, apply(): lax.all_to_all(jnp.stack([stacked.astype(jnp.bfloat16)] * lax.axis_size('...  108 us
    psum x1, blocking collectives, local(): lax.psum(jnp.stack([inner(primal, primal), inner(primal, tangent)]), ('ro...  81.9 us
    unnamed x73, local copies, waits for them, and re-layouts  59.9 us
  transfers between devices with their start and end apart: 9, of which 7 were waited for; matrix products, arithmetic and copies ran while one was open for 9% of the time, Pallas kernels for 0%

profile of v1, /device:TPU:1, one launch (start us, length us, event | category | flops | bytes accessed | tf_op | source)
XLA Modules:
  0.0 1130.2 jit_solution(890827312399497373)
XLA Ops:
  11.6 81.9 %psum.42 = f32[2]{0:T(128)S(1)} all-reduce(f32[2]{0:T(128)S(1)} %pad_maximum_fusion), channel_id=1, replica_groups=mesh['row'=16,'col'=16] {'row','col'}, use_global_device_ids=true, to_apply=%region_2.0 | all-reduce | flops 2 | bytes 16 | tf_op jit(solution)/shard_map/psum | solution.py:65
  98.3 4.7 all-to-all-start
  103.2 17.0 %all-to-all-done = bf16[16,2,8192]{2,1,0:T(2,128)(2,1)S(1)} async-done(((bf16[16,2,8192]{2,1,0:T(2,128)(2,1)}), bf16[16,2,8192]{2,1,0:T(2,128)(2,1)S(1)}, u32[]{:S(2)}, u32[]{:S(2)}) %all-to-all-start) | async-done | bytes 524320 | tf_op jit(solution)/shard_map/all_to_all | solution.py:41
  121.6 4.8 copy.74
  126.3 4.5 copy.75
  145.1 20.5 %all_to_all.30 = bf16[16,2,8192]{2,1,0:T(2,128)(2,1)} all-to-all(bf16[16,2,8192]{2,1,0:T(2,128)(2,1)} %reshape.603), channel_id=1, replica_groups=mesh['row'=16,'col'=16] {'row'}, dimensions={0} | all-to-all | bytes 1048576 | tf_op jit(solution)/shard_map/all_to_all | solution.py:41
  173.9 3.6 copy.84
  185.2 28.4 %reduce-scatter.19.cloned.1.call-done = f32[64,256]{1,0:T(8,128)} async-done(((f32[1024,256]{1,0:T(8,128)}), f32[64,256]{1,0:T(8,128)}) %reduce-scatter.19.cloned.1.call-update) | async-done | bytes 65552
  214.6 80.7 %reduce-scatter.21.cloned.1.call-done = f32[64,256]{1,0:T(8,128)} async-done(((f32[1024,256]{1,0:T(8,128)}), f32[64,256]{1,0:T(8,128)}) %reduce-scatter.21.cloned.1.call-update) | async-done | bytes 65552
  299.1 77.2 %psum.43 = f32[3]{0:T(128)S(1)} all-reduce(f32[3]{0:T(128)S(1)} %pad_maximum_fusion.1), channel_id=1, replica_groups=mesh['row'=16,'col'=16] {'row','col'}, use_global_device_ids=true, to_apply=%region_8.0 | all-reduce | flops 3 | bytes 24 | tf_op jit(solution)/shard_map/psum | solution.py:79
  380.9 73.3 %psum.44 = f32[2]{0:T(128)S(1)} all-reduce(f32[2]{0:T(128)S(1)} %pad_maximum_fusion.2), channel_id=1, replica_groups=mesh['row'=16,'col'=16] {'row','col'}, use_global_device_ids=true, to_apply=%region_11.0 | all-reduce | flops 2 | bytes 16 | tf_op jit(solution)/shard_map/psum | solution.py:94
  458.8 23.2 %all_to_all.31 = bf16[16,2,8192]{2,1,0:T(2,128)(2,1)} all-to-all(bf16[16,2,8192]{2,1,0:T(2,128)(2,1)} %reshape.607), channel_id=1, replica_groups=mesh['row'=16,'col'=16] {'row'}, dimensions={0} | all-to-all | bytes 1048576 | tf_op jit(solution)/shard_map/all_to_all | solution.py:41
  494.3 3.6 copy.90
  507.6 20.5 %all_to_all.32 = bf16[16,2,8192]{2,1,0:T(2,128)(2,1)} all-to-all(bf16[16,2,8192]{2,1,0:T(2,128)(2,1)} %reshape.605), channel_id=1, replica_groups=mesh['row'=16,'col'=16] {'row'}, dimensions={0} | all-to-all | bytes 1048576 | tf_op jit(solution)/shard_map/all_to_all | solution.py:41
  532.3 3.3 fusion.39
  540.4 3.6 copy.96
  551.6 24.8 %reduce-scatter.23.cloned.1.call-done = f32[64,256]{1,0:T(8,128)} async-done(((f32[1024,256]{1,0:T(8,128)}), f32[64,256]{1,0:T(8,128)}) %reduce-scatter.23.cloned.1.call-update) | async-done | bytes 65552
  577.4 80.8 %reduce-scatter.25.cloned.1.call-done = f32[64,256]{1,0:T(8,128)} async-done(((f32[1024,256]{1,0:T(8,128)}), f32[64,256]{1,0:T(8,128)}) %reduce-scatter.25.cloned.1.call-update) | async-done | bytes 65552
  660.1 3.9 stack.92
  664.0 77.2 %psum.45 = f32[6]{0:T(128)S(1)} all-reduce(f32[6]{0:T(128)S(1)} %stack.92), channel_id=1, replica_groups=mesh['row'=16,'col'=16] {'row','col'}, use_global_device_ids=true, to_apply=%region_20.0 | all-reduce | flops 6 | bytes 48 | tf_op jit(solution)/shard_map/psum | solution.py:79
  742.5 3.3 multiply_reduce_fusion.1
  747.1 73.3 %psum.46 = f32[2]{0:T(128)S(1)} all-reduce(f32[2]{0:T(128)S(1)} %pad_maximum_fusion.3), channel_id=1, replica_groups=mesh['row'=16,'col'=16] {'row','col'}, use_global_device_ids=true, to_apply=%region_23.0 | all-reduce | flops 2 | bytes 16 | tf_op jit(solution)/shard_map/psum | solution.py:94
  825.0 23.0 %all_to_all.33 = bf16[16,2,8192]{2,1,0:T(2,128)(2,1)} all-to-all(bf16[16,2,8192]{2,1,0:T(2,128)(2,1)} %reshape.609), channel_id=1, replica_groups=mesh['row'=16,'col'=16] {'row'}, dimensions={0} | all-to-all | bytes 1048576 | tf_op jit(solution)/shard_map/all_to_all | solution.py:41
  860.3 3.6 copy.108
  873.6 20.6 %all_to_all.34 = bf16[16,2,8192]{2,1,0:T(2,128)(2,1)} all-to-all(bf16[16,2,8192]{2,1,0:T(2,128)(2,1)} %reshape.611), channel_id=1, replica_groups=mesh['row'=16,'col'=16] {'row'}, dimensions={0} | all-to-all | bytes 1048576 | tf_op jit(solution)/shard_map/all_to_all | solution.py:41
  898.4 3.3 fusion.40
  906.5 3.6 copy.102
  920.3 22.2 %reduce-scatter.29.cloned.1.call-done = f32[64,256]{1,0:T(8,128)} async-done(((f32[1024,256]{1,0:T(8,128)}), f32[64,256]{1,0:T(8,128)}) %reduce-scatter.29.cloned.1.call-update) | async-done | bytes 65552
  943.5 80.9 %reduce-scatter.27.cloned.1.call-done = f32[64,256]{1,0:T(8,128)} async-done(((f32[1024,256]{1,0:T(8,128)}), f32[64,256]{1,0:T(8,128)}) %reduce-scatter.27.cloned.1.call-update) | async-done | bytes 65552
  1026.5 5.8 stack.107
  1032.3 77.2 %psum.47 = f32[9]{0:T(128)S(1)} all-reduce(f32[9]{0:T(128)S(1)} %stack.107), channel_id=1, replica_groups=mesh['row'=16,'col'=16] {'row','col'}, use_global_device_ids=true, to_apply=%region_35.0 | all-reduce | flops 9 | bytes 72 | tf_op jit(solution)/shard_map/psum | solution.py:79
  1117.5 3.9 multiply_add_fusion
  (210 shorter events, 151.5 us)
Async XLA Ops:
  7.2 114.4 %all-gather.3.cloned.1.call-start = ((), (), s32[]{:S(2)}) async-start(), calls=%async_computation.12 | async-start | bytes 2228224 | tf_op jit(solution)/shard_map/all_gather | solution.py:35
  7.9 129.2 %all-gather.5.cloned.1.call-start = ((), (), s32[]{:S(2)}) async-start(), calls=%async_computation.13 | async-start | bytes 2228224 | tf_op jit(solution)/shard_map/all_gather | solution.py:36
  10.2 92.9 %copy-start.10 = (bf16[16,16,4,4]{1,3,2,0:T(4,128)(2,1)S(1)}, bf16[16,16,4,4]{1,3,2,0:T(4,128)(2,1)}, u32[]{:S(2)}) copy-start(bf16[16,16,4,4]{1,3,2,0:T(4,128)(2,1)} %param.32) | copy-start | bytes 24580
  98.3 21.9 %all-to-all-start = ((bf16[16,2,8192]{2,1,0:T(2,128)(2,1)}), bf16[16,2,8192]{2,1,0:T(2,128)(2,1)S(1)}, u32[]{:S(2)}, u32[]{:S(2)}) async-start(bf16[16,2,8192]{2,1,0:T(2,128)(2,1)} %reshape.601), calls=%async_computation | async-start | bytes 1048576 | tf_op jit(solution)/shard_map/all_to_all | solution.py:41
  103.0 110.5 %reduce-scatter.19.cloned.1.call-start = ((), (), s32[]{:S(2)}) async-start(), calls=%async_computation.14 | async-start | bytes 1114112
  103.2 68.8 %copy-start.11 = (bf16[16,16,4,4]{0,1,2,3:T(8,128)(2,1)}, bf16[16,16,4,4]{0,1,2,3:T(8,128)(2,1)S(1)}, u32[]{:S(2)}) copy-start(bf16[16,16,4,4]{0,1,2,3:T(8,128)(2,1)S(1)} %copy.77) | copy-start | bytes 24580
  130.8 1.5 copy-start.5
  143.1 152.2 %reduce-scatter.21.cloned.1.call-start = ((), (), s32[]{:S(2)}) async-start(), calls=%async_computation.15 | async-start | bytes 1114112
  145.1 24.7 %copy-start.6 = (bf16[64,1024,16]{1,0,2:T(8,128)(2,1)S(1)}, bf16[64,1024,16]{1,0,2:T(8,128)(2,1)}, u32[]{:S(2)}) copy-start(bf16[64,1024,16]{1,0,2:T(8,128)(2,1)} %copy-done.5) | copy-start | bytes 6291460
  172.0 5.6 copy-start
  181.8 114.5 %copy-start.1 = (bf16[64,4,64]{2,1,0:T(4,128)(2,1)S(1)}, bf16[64,4,64]{2,1,0:T(4,128)(2,1)}, u32[]{:S(2)}) copy-start(bf16[64,4,64]{2,1,0:T(4,128)(2,1)} %param.28) | copy-start | bytes 98308
  181.8 114.6 %copy-start.2 = (bf16[64,4,64]{2,1,0:T(4,128)(2,1)S(1)}, bf16[64,4,64]{2,1,0:T(4,128)(2,1)}, u32[]{:S(2)}) copy-start(bf16[64,4,64]{2,1,0:T(4,128)(2,1)} %param.29) | copy-start | bytes 98308
  181.8 114.6 %copy-start.12 = (f32[4]{0:T(128)S(1)}, f32[4]{0:T(128)}, u32[]{:S(2)}) copy-start(f32[4]{0:T(128)} %param.33) | copy-start | bytes 52
  185.1 391.2 %reduce-scatter.23.cloned.1.call-start = ((), (), s32[]{:S(2)}) async-start(), calls=%async_computation.16 | async-start | bytes 1114112
  502.2 3.3 copy-start.8
  505.5 152.7 %reduce-scatter.25.cloned.1.call-start = ((), (), s32[]{:S(2)}) async-start(), calls=%async_computation.17 | async-start | bytes 1114112
  551.6 390.9 %reduce-scatter.29.cloned.1.call-start = ((), (), s32[]{:S(2)}) async-start(), calls=%async_computation.19 | async-start | bytes 1114112
  745.8 77.2 %copy-start.3 = (f32[64,4,64]{2,0,1:T(8,128)}, f32[64,4,64]{2,0,1:T(8,128)S(1)}, u32[]{:S(2)}) copy-start(f32[64,4,64]{2,0,1:T(8,128)S(1)} %get-tuple-element.171) | copy-start | bytes 196612
  868.3 3.3 copy-start.9
  871.5 152.9 %reduce-scatter.27.cloned.1.call-start = ((), (), s32[]{:S(2)}) async-start(), calls=%async_computation.18 | async-start | bytes 1114112
  913.6 111.9 %copy-start.4 = (f32[64,4,64]{2,0,1:T(8,128)S(1)}, f32[64,4,64]{2,0,1:T(8,128)}, u32[]{:S(2)}) copy-start(f32[64,4,64]{2,0,1:T(8,128)} %copy-done.3) | copy-start | bytes 196612
  913.6 111.9 %copy-start.7 = (f32[64,4,64]{2,0,1:T(8,128)S(1)}, f32[64,4,64]{2,0,1:T(8,128)}, u32[]{:S(2)}) copy-start(f32[64,4,64]{2,0,1:T(8,128)} %get-tuple-element.169) | copy-start | bytes 196612
  915.8 194.0 %copy-start.13 = (f32[3,1]{0,1:T(1,128)S(1)}, f32[3,1]{0,1:T(1,128)}, u32[]{:S(2)}) copy-start(f32[3,1]{0,1:T(1,128)} %constant.327) | copy-start | bytes 40
Sparse Core Ops, SparseCore 0:
  10.5 52.1 all-gather.2
  64.5 40.7 all-gather.4
  143.2 70.3 reduce-scatter.18
  216.9 78.3 reduce-scatter.20
  505.6 70.6 reduce-scatter.22
  579.7 78.4 reduce-scatter.24
  871.7 70.7 reduce-scatter.28
  945.9 78.4 reduce-scatter.26
